TPU v7x, 512 devices: a whole 4x4x16 slice. The times are simulated.
512 devices in a mesh: blk: 16 (over x_hi, y, core), wide: 32 (over x_lo, z).
Axes of the slice: x: 4 (x_hi: 2, x_lo: 2; x = x_hi * 2 + x_lo), y: 4, z: 16, core: 2. Of those that a mesh axis runs over, the one named last changes fastest.
Arguments:
- series: bfloat16 [90112, 640], P(('blk', 'wide'))
- scrub_mask: int32 [640], replicated, may hold values from 0 to 1, as said below
- seed_index: int32 [4096], P(('blk', 'wide')), may hold values from 0 to 90111, as said below
Outputs:
- dispersion: bfloat16 [16, 5632, 4096], P(None, 'wide', 'blk')
- statistic: bfloat16 [16, 5632, 4096], P(None, 'wide', 'blk')
Inputs may be any that keep to these rules, and one draw needn't show every extreme that they name: Entry i of seed_index lies among the rows (i // 8) * 176 to (i // 8 + 1) * 176 - 1, and the 8 entries of one such block are distinct. `scrub_mask`: every frame of even position is kept.
All inputs are finite; a program needn't handle non-finite values.
Results may differ from a plain program's by a relative error of at most 0.0057.
Values may be sent and summed in bfloat16 or wider, within the bound.
No kernel may reach another device: no remote copies, remote signals or barrier semaphores. Data moves between devices by JAX's collectives and lax.ppermute only.
A program may use at most 128 MiB of HBM per device.

v0:
```python
import jax
import jax.numpy as jnp
from jax import lax
from jax.sharding import PartitionSpec as P

WIN = 60
STRIDE = 30
NWIN = 20
EPSILON = 1e-05
CLIP_LEVEL = 0.99


def fisher_of(values):
    clipped = jnp.clip(values, -CLIP_LEVEL, CLIP_LEVEL)
    return 0.5 * (jnp.log(1.0 + clipped) - jnp.log(1.0 - clipped))


def prepare(raw_rows, scrub_mask):
    values = raw_rows.astype(jnp.float32)
    row_count = values.shape[0]
    weight = scrub_mask.astype(jnp.float32)
    covered = STRIDE * (NWIN + 1)
    pieces = values[:, :covered].reshape(row_count, NWIN + 1, STRIDE)
    framed = jnp.concatenate([pieces[:, :-1], pieces[:, 1:]], axis=2)
    mask_pieces = weight[:covered].reshape(NWIN + 1, STRIDE)
    mask_framed = jnp.concatenate([mask_pieces[:-1], mask_pieces[1:]], axis=1)
    valid_count = jnp.sum(mask_framed, axis=1)
    centre = jnp.sum(framed * mask_framed, axis=2) / valid_count
    centred = (framed - centre[:, :, None]) * mask_framed
    spread = jnp.sum(centred * centred, axis=2)
    windows = (centred * lax.rsqrt(spread + EPSILON)[:, :, None]).astype(jnp.bfloat16)
    total_valid = jnp.sum(weight)
    mean_all = jnp.sum(values * weight, axis=1) / total_valid
    centred_all = (values - mean_all[:, None]) * weight
    spread_all = jnp.sum(centred_all * centred_all, axis=1)
    whole_std = (centred_all * lax.rsqrt(spread_all + EPSILON)[:, None]).astype(jnp.bfloat16)
    return (windows, whole_std)


def compare(target_windows, target_whole, seed_window, seed_whole, total_valid):
    window_corr = jnp.einsum(
        "tnw,snw->nts", target_windows, seed_window, preferred_element_type=jnp.float32
    )
    fisher = fisher_of(window_corr)
    first_moment = jnp.mean(fisher, axis=0)
    second = jnp.mean(fisher * fisher, axis=0)
    dispersion = ((WIN - 3) * (second - first_moment * first_moment)).astype(jnp.bfloat16)
    static = jnp.einsum("tf,sf->ts", target_whole, seed_whole, preferred_element_type=jnp.float32)
    statistic = (jnp.sqrt(total_valid - 3.0) * fisher_of(static)).astype(jnp.bfloat16)
    return (dispersion, statistic)


def body(series, scrub_mask, seed_index):
    row_count, frames = series.shape
    local_rows = seed_index % row_count
    own_seeds = jnp.take(series, local_rows, axis=0)
    total_valid = jnp.sum(scrub_mask.astype(jnp.float32))
    panel_rows = lax.all_gather(own_seeds, "wide", axis=0, tiled=True)
    seed_window, seed_whole = prepare(panel_rows, scrub_mask)
    blocks = lax.axis_size("blk")
    gathered = lax.all_gather(series, "blk", axis=0, tiled=True)
    target_windows, target_whole = prepare(gathered, scrub_mask)
    dispersion, statistic = compare(
        target_windows, target_whole, seed_window, seed_whole, total_valid
    )
    shape = (blocks, row_count, panel_rows.shape[0])
    return (dispersion.reshape(shape), statistic.reshape(shape))


def solution(mesh):
    in_specs = (P(("blk", "wide"), None), P(), P(("blk", "wide")))
    out_specs = (P(None, "wide", "blk"), P(None, "wide", "blk"))
    return jax.shard_map(body, mesh=mesh, in_specs=in_specs, out_specs=out_specs, check_vma=False)
```

profile of v0, /device:TPU:24, one launch (start us, length us, event | category | flops | bytes accessed | tf_op | source)
XLA Modules:
  0.0 186.0 jit_solution(18207394981131811877)
XLA Ops:
  7.2 0.0 all-gather.2.cloned.1.call-start
  7.2 0.7 all-gather.2.cloned.1.call-update
  7.9 0.7 convert_element_type.29
  8.6 1.3 convert_reduce_fusion
  10.6 0.7 compare_and_fusion
  11.3 1.5 gather_fusion
  12.8 0.1 fusion.17
  12.9 0.1 slice.44
  13.0 0.1 slice.46
  13.1 0.1 reduce_sum.132
  13.2 0.1 reduce_sum.133
  13.3 0.1 broadcast_select_fusion
  13.4 70.7 %all_gather.7 = bf16[256,640]{1,0:T(8,128)(2,1)S(1)} all-gather(bf16[8,640]{1,0:T(8,128)(2,1)S(1)} %broadcast_select_fusion), channel_id=1, replica_groups=mesh['blk'=16,'wide'=32] {'wide'}, dimensions={0}, use_global_device_ids=true | all-gather | bytes 337920 | tf_op jit(solution)/shard_map/all_gather | solution.py:58
  84.1 0.2 copy.10
  84.4 0.1 reshape.98
  84.5 0.1 pad_maximum_fusion.2
  84.5 0.1 multiply_reduce_fusion.8
  84.7 0.7 broadcast_divide_fusion.3
  85.3 0.2 multiply_reduce_fusion.7
  85.6 0.2 fusion.16
  85.7 0.3 multiply_reduce_fusion.6
  86.1 0.1 broadcast_divide_fusion.1
  86.2 0.5 multiply_reduce_fusion.5
  86.7 0.0 all-gather.2.cloned.1.call-done
  86.7 0.0 copy-start.2
  86.7 3.0 %multiply_reduce_fusion.4 = f32[2816]{0:T(1024)S(1)} fusion(bf16[2816,640]{1,0:T(8,128)(2,1)} %all-gather.2.cloned.1.call-done, f32[640]{0:T(1024)S(1)} %convert_element_type.29), kind=kLoop, calls=%fused_computation.13 | loop fusion | flops 5403904 | bytes 3618304 | tf_op jit(solution)/shard_map/reduce_sum | solution.py:33
  89.7 0.7 broadcast_divide_fusion.2
  90.3 3.8 %multiply_reduce_fusion.3 = f32[2816]{0:T(1024)S(1)} fusion(bf16[2816,640]{1,0:T(8,128)(2,1)} %all-gather.2.cloned.1.call-done, f32[2816]{0:T(1024)S(1)} %broadcast_divide_fusion.2, f32[640]{0:T(1024)S(1)} %convert_element_type.29), kind=kLoop, calls=%fused_computation.11 | loop fusion | flops 9008384 | bytes 3629568 | tf_op jit(solution)/shard_map/reduce_sum | solution.py:35
  94.1 0.0 copy-done.2
  94.1 3.4 %slice.52 = f32[2816,630]{1,0:T(8,128)} slice(bf16[2816,640]{1,0:T(8,128)(2,1)S(1)} %copy-done.2), slice={[0:2816], [0:630]} | slice | bytes 14192640 | tf_op jit(solution)/shard_map/slice | solution.py:23
  97.5 8.6 %copy.9 = f32[2816,630]{0,1:T(8,128)} copy(f32[2816,630]{1,0:T(8,128)} %slice.52) | data formatting | bytes 14192640 | tf_op jit(solution)/shard_map/slice | solution.py:23
  106.1 7.9 %reshape.97 = f32[2816,21,30]{0,2,1:T(8,128)} reshape(f32[2816,630]{0,1:T(8,128)} %copy.9) | data formatting | bytes 14192640 | tf_op jit(solution)/shard_map/reshape | solution.py:23
  114.0 11.9 %fusion.15 = (f32[2816,20,30]{0,2,1:T(8,128)}, f32[2816,20,30]{0,2,1:T(8,128)}) fusion(f32[2816,21,30]{0,2,1:T(8,128)} %reshape.97), kind=kLoop, calls=%fused_computation.54 | loop fusion | bytes 27033600 | tf_op jit(solution)/shard_map/slice | solution.py:24
  125.9 0.0 copy-start
  125.9 0.0 copy-start.1
  125.9 8.0 %multiply_reduce_fusion.2 = f32[2816,20]{0,1:T(8,128)S(1)} fusion(f32[2816,20,30]{0,2,1:T(8,128)} %get-tuple-element.7, f32[2816,20,30]{0,2,1:T(8,128)} %get-tuple-element.6, f32[20,60]{1,0:T(8,128)S(1)} %pad_maximum_fusion.2), kind=kLoop, calls=%fused_computation.8 | loop fusion | flops 10081280 | bytes 13746880 | tf_op jit(solution)/shard_map/reduce_sum | solution.py:28
  133.9 0.1 broadcast_divide_fusion
  134.0 0.0 copy-done
  134.0 1.2 copy-done.1
  135.3 3.5 %multiply_reduce_fusion.1 = f32[2816,20]{0,1:T(8,128)S(1)} fusion(f32[2816,20,30]{0,2,1:T(8,128)S(1)} %copy-done.1, f32[2816,20,30]{0,2,1:T(8,128)S(1)} %copy-done, f32[2816,20]{0,1:T(8,128)S(1)} %broadcast_divide_fusion, f32[20,60]{1,0:T(8,128)S(1)} %pad_maximum_fusion.2), kind=kLoop, calls=%fused_computation.6 | loop fusion | flops 16839680 | bytes 13972160 | tf_op jit(solution)/shard_map/reduce_sum | solution.py:30
  138.8 32.3 %multiply_reduce_fusion = (f32[2816,256]{1,0:T(8,128)}, f32[2816,256]{1,0:T(8,128)}) fusion(f32[256,20,30]{0,2,1:T(8,128)S(1)} %get-tuple-element.9, f32[256,20,30]{0,2,1:T(8,128)S(1)} %get-tuple-element.8, f32[256,20]{0,1:T(8,128)S(1)} %add_rsqrt_fusion.1, f32[256,20]{0,1:T(8,128)S(1)} %broadcast_divide_fusion.1, f32[20,60]{1,0:T(8,128)S(1)} %pad_maximum_fusion.2, ...), kind=kOutput, calls=%fused_computation.1 | convolution fusion | flops 1862483968 | bytes 21009088 | tf_op jit(solution)/shard_map/tnw,snw->nts/dot_general | solution.py:41
  171.1 0.0 copy-start.3
  171.1 4.5 %multiply_convert_fusion.7 = bf16[2816,256]{1,0:T(8,128)(2,1)} fusion(f32[2816,256]{1,0:T(8,128)} %get-tuple-element.3, f32[2816,256]{1,0:T(8,128)} %get-tuple-element.2), kind=kLoop, calls=%fused_computation.22 | loop fusion | flops 4325376 | bytes 7208960 | tf_op jit(solution)/shard_map/convert
  175.6 0.0 copy-done.3
  175.6 3.6 %multiply_convert_fusion.4 = bf16[2816,256]{1,0:T(8,128)(2,1)} fusion(bf16[2816,640]{1,0:T(8,128)(2,1)S(1)} %copy-done.3, f32[2816]{0:T(1024)S(1)} %add_rsqrt_fusion.2, f32[2816]{0:T(1024)S(1)} %broadcast_divide_fusion.2, f32[640]{0:T(1024)S(1)} %convert_element_type.29, f32[]{:T(128)S(6)} %mul.165, bf16[256,640]{1,0:T(8,128)(2,1)S(1)} %all_gather.7, ...), kind=kOutput, calls=%fused_computation.21 | convolution fusion | flops 936902656 | bytes 5401092 | tf_op jit(solution)/shard_map/tf,sf->ts/dot_general | solution.py:48
  (7 shorter events, 0.1 us)
Async XLA Ops:
  7.2 79.5 %all-gather.2.cloned.1.call-start = ((), (), s32[]{:S(2)}) async-start(), calls=%async_computation | async-start | bytes 3829760 | tf_op jit(solution)/shard_map/all_gather | solution.py:61
  86.7 7.4 %copy-start.2 = (bf16[2816,640]{1,0:T(8,128)(2,1)S(1)}, bf16[2816,640]{1,0:T(8,128)(2,1)}, u32[]{:S(2)}) copy-start(bf16[2816,640]{1,0:T(8,128)(2,1)} %all-gather.2.cloned.1.call-done) | copy-start | bytes 10813444
  125.9 8.1 %copy-start = (f32[2816,20,30]{0,2,1:T(8,128)S(1)}, f32[2816,20,30]{0,2,1:T(8,128)}, u32[]{:S(2)}) copy-start(f32[2816,20,30]{0,2,1:T(8,128)} %get-tuple-element.6) | copy-start | bytes 20275204
  125.9 9.4 %copy-start.1 = (f32[2816,20,30]{0,2,1:T(8,128)S(1)}, f32[2816,20,30]{0,2,1:T(8,128)}, u32[]{:S(2)}) copy-start(f32[2816,20,30]{0,2,1:T(8,128)} %get-tuple-element.7) | copy-start | bytes 20275204
  171.1 4.5 %copy-start.3 = (bf16[2816,640]{1,0:T(8,128)(2,1)S(1)}, bf16[2816,640]{1,0:T(8,128)(2,1)}, u32[]{:S(2)}) copy-start(bf16[2816,640]{1,0:T(8,128)(2,1)} %all-gather.2.cloned.1.call-done) | copy-start | bytes 10813444
Sparse Core Ops, SparseCore 0:
  11.2 71.5 all-gather.1
where the time goes:
time: 187 us; the launch traced here: 186 us
  blocking collectives  70.7 us (38%)
  matrix products  35.9 us (19%)
  local copies, waits for them, and re-layouts  35.3 us (19%)
  other arithmetic  28.5 us (15%)
  between operations  14.9 us (8%)
    all_gather x1, blocking collectives, body(): panel_rows = lax.all_gather(own_seeds, 'wide', axis=0, tiled=True)  70.7 us
    dot_general x1, matrix products, compare(): jnp.einsum('tnw,snw->nts', target_windows, seed_window, preferred_element...  32.3 us
    slice x4, local copies, waits for them, and re-layouts, prepare(): pieces = values[:, :covered].reshape(row_count, NWIN + 1, STRIDE)  12.3 us
    slice x2, local copies, waits for them, and re-layouts, prepare(): framed = jnp.concatenate([pieces[:, :-1], pieces[:, 1:]], axis=2)  12 us
    reduce_sum x2, other arithmetic, prepare(): centre = jnp.sum(framed * mask_framed, axis=2) / valid_count  8.33 us
    reshape x2, local copies, waits for them, and re-layouts, prepare(): pieces = values[:, :covered].reshape(row_count, NWIN + 1, STRIDE)  7.96 us
    another operation x1, other arithmetic  4.49 us
    reduce_sum x2, other arithmetic, prepare(): spread_all = jnp.sum(centred_all * centred_all, axis=1)  4.02 us
  transfers between devices with their start and end apart: 1, of which 0 were waited for; matrix products, arithmetic and copies ran while one was open for 4% of the time, Pallas kernels for 0%

commit v1 on v0

--- a/solution.py
+++ b/solution.py
@@ -55,7 +55,9 @@
     local_rows = seed_index % row_count
     own_seeds = jnp.take(series, local_rows, axis=0)
     total_valid = jnp.sum(scrub_mask.astype(jnp.float32))
-    panel_rows = lax.all_gather(own_seeds, "wide", axis=0, tiled=True)
+    panel_rows = jnp.concatenate(
+        lax.all_to_all(jnp.stack([own_seeds] * lax.axis_size("wide")), "wide", 0, 0), axis=0
+    )
     seed_window, seed_whole = prepare(panel_rows, scrub_mask)
     blocks = lax.axis_size("blk")
     gathered = lax.all_gather(series, "blk", axis=0, tiled=True)

time: 187 us -> 185 us (0.989)
  blocking collectives: 70.7 us -> 0 us
  waiting for transfers between devices: 0.7 us -> 50.4 us
  starting transfers between devices: 0.04 us -> 16.4 us
    all_gather x1 -> x0, blocking collectives: 70.7 us -> none  [body(): panel_rows = lax.all_gather(own_seeds, 'wide', axis=0, tiled=True)]
    all_gather x1, waiting for transfers between devices: 0.02 us -> 28.2 us  [body(): gathered = lax.all_gather(series, 'blk', axis=0, tiled=True)]
    all_to_all x0 -> x1, waiting for transfers between devices: none -> 21.6 us  [body(): lax.all_to_all(jnp.stack([own_seeds] * lax.axis_size('wide')), 'wide', 0, 0)]
    all_to_all x0 -> x1, starting transfers between devices: none -> 16.4 us  [body(): lax.all_to_all(jnp.stack([own_seeds] * lax.axis_size('wide')), 'wide', 0, 0)]
    slice x4 -> x3, local copies, waits for them, and re-layouts: 12.3 us -> 12.2 us  [prepare(): pieces = values[:, :covered].reshape(row_count, NWIN + 1, STRIDE)]
  transfers between devices with their start and end apart: 1 -> 2, of which waited for: 0 -> 2; matrix products, arithmetic and copies ran while one was open for 4% -> 4% of each run, Pallas kernels for 0% -> 0%
where the time goes in v1:
time: 185 us; the launch traced here: 182 us
  waiting for transfers between devices  50.4 us (27%)
  local copies, waits for them, and re-layouts  36.2 us (20%)
  matrix products  36.1 us (20%)
  other arithmetic  28.3 us (15%)
  starting transfers between devices  16.4 us (9%)
  between operations  14.9 us (8%)
    dot_general x1, matrix products, compare(): jnp.einsum('tnw,snw->nts', target_windows, seed_window, preferred_element...  32.5 us
    all_gather x1, waiting for transfers between devices, body(): gathered = lax.all_gather(series, 'blk', axis=0, tiled=True)  28.2 us
    all_to_all x1, waiting for transfers between devices, body(): lax.all_to_all(jnp.stack([own_seeds] * lax.axis_size('wide')), 'wide', 0, 0)  21.6 us
    all_to_all x1, starting transfers between devices, body(): lax.all_to_all(jnp.stack([own_seeds] * lax.axis_size('wide')), 'wide', 0, 0)  16.4 us
    slice x3, local copies, waits for them, and re-layouts, prepare(): pieces = values[:, :covered].reshape(row_count, NWIN + 1, STRIDE)  12.2 us
    slice x2, local copies, waits for them, and re-layouts, prepare(): framed = jnp.concatenate([pieces[:, :-1], pieces[:, 1:]], axis=2)  12 us
    reduce_sum x2, other arithmetic, prepare(): centre = jnp.sum(framed * mask_framed, axis=2) / valid_count  8.32 us
    reshape x2, local copies, waits for them, and re-layouts, prepare(): pieces = values[:, :covered].reshape(row_count, NWIN + 1, STRIDE)  7.96 us
  transfers between devices with their start and end apart: 2, of which 2 were waited for; matrix products, arithmetic and copies ran while one was open for 4% of the time, Pallas kernels for 0%

profile of v1, /device:TPU:24, one launch (start us, length us, event | category | flops | bytes accessed | tf_op | source)
XLA Modules:
  0.0 182.3 jit_solution(16849584445205467434)
XLA Ops:
  7.2 0.0 all-gather.2.cloned.1.call-start
  7.2 0.7 all-gather.2.cloned.1.call-update
  7.9 0.7 compare_and_fusion
  8.6 1.5 gather_fusion
  10.1 0.1 broadcast_select_fusion
  10.2 0.8 stack.2
  11.0 16.4 %all-to-all-start = ((bf16[32,8,640]{2,1,0:T(8,128)(2,1)}), bf16[32,8,640]{2,1,0:T(8,128)(2,1)S(1)}, u32[]{:S(2)}, u32[]{:S(2)}) async-start(bf16[32,8,640]{2,1,0:T(8,128)(2,1)} %stack.2), calls=%async_computation | async-start | bytes 655360 | tf_op jit(solution)/shard_map/all_to_all | solution.py:59
  27.4 0.7 convert_element_type.36
  28.1 1.3 convert_reduce_fusion
  30.1 0.1 fusion.21
  30.1 0.1 slice.44
  30.2 0.1 slice.46
  30.3 0.1 reduce_sum.132
  30.4 0.1 reduce_sum.133
  30.5 0.1 pad_maximum_fusion.2
  30.6 21.6 %all-to-all-done = bf16[32,8,640]{2,1,0:T(8,128)(2,1)S(1)} async-done(((bf16[32,8,640]{2,1,0:T(8,128)(2,1)}), bf16[32,8,640]{2,1,0:T(8,128)(2,1)S(1)}, u32[]{:S(2)}, u32[]{:S(2)}) %all-to-all-start) | async-done | bytes 327712 | tf_op jit(solution)/shard_map/all_to_all | solution.py:59
  52.2 0.1 fusion.8
  52.3 0.7 broadcast_divide_fusion.2
  53.0 0.1 div.64
  53.1 0.2 fusion.11
  53.3 0.1 rsqrt.35
  53.5 0.2 copy.12
  53.7 0.1 reshape.135
  53.8 0.1 fusion.20
  54.0 0.3 multiply_reduce_fusion.6
  54.3 0.1 broadcast_divide_fusion.1
  54.4 0.5 multiply_reduce_fusion.5
  54.9 28.2 %all-gather.2.cloned.1.call-done = bf16[2816,640]{1,0:T(8,128)(2,1)} async-done(((bf16[176,640]{1,0:T(8,128)(2,1)}), bf16[2816,640]{1,0:T(8,128)(2,1)}) %all-gather.2.cloned.1.call-update) | async-done | bytes 3604496 | tf_op jit(solution)/shard_map/all_gather | solution.py:63
  83.0 0.0 copy-start.2
  83.0 2.9 %multiply_reduce_fusion.4 = f32[2816]{0:T(1024)S(1)} fusion(bf16[2816,640]{1,0:T(8,128)(2,1)} %all-gather.2.cloned.1.call-done, f32[640]{0:T(1024)S(1)} %convert_element_type.36), kind=kLoop, calls=%fused_computation.13 | loop fusion | flops 5403904 | bytes 3618304 | tf_op jit(solution)/shard_map/reduce_sum | solution.py:33
  86.0 0.7 broadcast_divide_fusion.3
  86.7 3.6 %multiply_reduce_fusion.3 = f32[2816]{0:T(1024)S(1)} fusion(bf16[2816,640]{1,0:T(8,128)(2,1)} %all-gather.2.cloned.1.call-done, f32[2816]{0:T(1024)S(1)} %broadcast_divide_fusion.3, f32[640]{0:T(1024)S(1)} %convert_element_type.36), kind=kLoop, calls=%fused_computation.11 | loop fusion | flops 9008384 | bytes 3629568 | tf_op jit(solution)/shard_map/reduce_sum | solution.py:35
  90.3 0.0 copy-done.2
  90.3 3.4 %slice.52 = f32[2816,630]{1,0:T(8,128)} slice(bf16[2816,640]{1,0:T(8,128)(2,1)S(1)} %copy-done.2), slice={[0:2816], [0:630]} | slice | bytes 14192640 | tf_op jit(solution)/shard_map/slice | solution.py:23
  93.7 8.6 %copy.11 = f32[2816,630]{0,1:T(8,128)} copy(f32[2816,630]{1,0:T(8,128)} %slice.52) | data formatting | bytes 14192640 | tf_op jit(solution)/shard_map/slice | solution.py:23
  102.3 7.9 %reshape.134 = f32[2816,21,30]{0,2,1:T(8,128)} reshape(f32[2816,630]{0,1:T(8,128)} %copy.11) | data formatting | bytes 14192640 | tf_op jit(solution)/shard_map/reshape | solution.py:23
  110.2 11.9 %fusion.19 = (f32[2816,20,30]{0,2,1:T(8,128)}, f32[2816,20,30]{0,2,1:T(8,128)}) fusion(f32[2816,21,30]{0,2,1:T(8,128)} %reshape.134), kind=kLoop, calls=%fused_computation.58 | loop fusion | bytes 27033600 | tf_op jit(solution)/shard_map/slice | solution.py:24
  122.1 0.0 copy-start
  122.1 0.0 copy-start.1
  122.1 8.0 %multiply_reduce_fusion.2 = f32[2816,20]{0,1:T(8,128)S(1)} fusion(f32[2816,20,30]{0,2,1:T(8,128)} %get-tuple-element.7, f32[2816,20,30]{0,2,1:T(8,128)} %get-tuple-element.6, f32[20,60]{1,0:T(8,128)S(1)} %pad_maximum_fusion.2), kind=kLoop, calls=%fused_computation.8 | loop fusion | flops 10081280 | bytes 13746880 | tf_op jit(solution)/shard_map/reduce_sum | solution.py:28
  130.1 0.1 broadcast_divide_fusion
  130.2 0.0 copy-done
  130.2 1.2 copy-done.1
  131.4 3.5 %multiply_reduce_fusion.1 = f32[2816,20]{0,1:T(8,128)S(1)} fusion(f32[2816,20,30]{0,2,1:T(8,128)S(1)} %copy-done.1, f32[2816,20,30]{0,2,1:T(8,128)S(1)} %copy-done, f32[2816,20]{0,1:T(8,128)S(1)} %broadcast_divide_fusion, f32[20,60]{1,0:T(8,128)S(1)} %pad_maximum_fusion.2), kind=kLoop, calls=%fused_computation.6 | loop fusion | flops 16839680 | bytes 13972160 | tf_op jit(solution)/shard_map/reduce_sum | solution.py:30
  134.9 32.5 %multiply_reduce_fusion = (f32[2816,256]{1,0:T(8,128)}, f32[2816,256]{1,0:T(8,128)}) fusion(f32[256,20,30]{0,2,1:T(8,128)S(1)} %get-tuple-element.9, f32[256,20,30]{0,2,1:T(8,128)S(1)} %get-tuple-element.8, f32[256,20]{0,1:T(8,128)S(1)} %add_rsqrt_fusion.1, f32[256,20]{0,1:T(8,128)S(1)} %broadcast_divide_fusion.1, f32[20,60]{1,0:T(8,128)S(1)} %pad_maximum_fusion.2, ...), kind=kOutput, calls=%fused_computation.1 | convolution fusion | flops 1862483968 | bytes 21009088 | tf_op jit(solution)/shard_map/tnw,snw->nts/dot_general | solution.py:41
  167.4 0.0 copy-start.3
  167.4 4.5 %multiply_convert_fusion.7 = bf16[2816,256]{1,0:T(8,128)(2,1)} fusion(f32[2816,256]{1,0:T(8,128)} %get-tuple-element.3, f32[2816,256]{1,0:T(8,128)} %get-tuple-element.2), kind=kLoop, calls=%fused_computation.22 | loop fusion | flops 4325376 | bytes 7208960 | tf_op jit(solution)/shard_map/convert.1
  171.9 0.0 copy-done.3
  171.9 3.6 %multiply_convert_fusion.4 = bf16[2816,256]{1,0:T(8,128)(2,1)} fusion(bf16[2816,640]{1,0:T(8,128)(2,1)S(1)} %copy-done.3, f32[2816]{0:T(1024)S(1)} %add_rsqrt_fusion.3, f32[2816]{0:T(1024)S(1)} %broadcast_divide_fusion.3, f32[640]{0:T(1024)S(1)} %convert_element_type.36, f32[]{:T(128)S(6)} %mul.174, f32[256]{0:T(256)S(1)} %rsqrt.35, f32[256]{0:T(256)S(1)} %div.64, ...), kind=kOutput, calls=%fused_computation.21 | convolution fusion | flops 936902656 | bytes 5401092 | tf_op jit(solution)/shard_map/tf,sf->ts/dot_general | solution.py:48
  (7 shorter events, 0.1 us)
Async XLA Ops:
  7.2 75.9 %all-gather.2.cloned.1.call-start = ((), (), s32[]{:S(2)}) async-start(), calls=%async_computation.1 | async-start | bytes 3829760 | tf_op jit(solution)/shard_map/all_gather | solution.py:63
  11.0 41.2 %all-to-all-start = ((bf16[32,8,640]{2,1,0:T(8,128)(2,1)}), bf16[32,8,640]{2,1,0:T(8,128)(2,1)S(1)}, u32[]{:S(2)}, u32[]{:S(2)}) async-start(bf16[32,8,640]{2,1,0:T(8,128)(2,1)} %stack.2), calls=%async_computation | async-start | bytes 655360 | tf_op jit(solution)/shard_map/all_to_all | solution.py:59
  83.0 7.2 %copy-start.2 = (bf16[2816,640]{1,0:T(8,128)(2,1)S(1)}, bf16[2816,640]{1,0:T(8,128)(2,1)}, u32[]{:S(2)}) copy-start(bf16[2816,640]{1,0:T(8,128)(2,1)} %all-gather.2.cloned.1.call-done) | copy-start | bytes 10813444
  122.1 8.1 %copy-start = (f32[2816,20,30]{0,2,1:T(8,128)S(1)}, f32[2816,20,30]{0,2,1:T(8,128)}, u32[]{:S(2)}) copy-start(f32[2816,20,30]{0,2,1:T(8,128)} %get-tuple-element.6) | copy-start | bytes 20275204
  122.1 9.4 %copy-start.1 = (f32[2816,20,30]{0,2,1:T(8,128)S(1)}, f32[2816,20,30]{0,2,1:T(8,128)}, u32[]{:S(2)}) copy-start(f32[2816,20,30]{0,2,1:T(8,128)} %get-tuple-element.7) | copy-start | bytes 20275204
  167.4 4.5 %copy-start.3 = (bf16[2816,640]{1,0:T(8,128)(2,1)S(1)}, bf16[2816,640]{1,0:T(8,128)(2,1)}, u32[]{:S(2)}) copy-start(bf16[2816,640]{1,0:T(8,128)(2,1)} %all-gather.2.cloned.1.call-done) | copy-start | bytes 10813444
Sparse Core Ops, SparseCore 0:
  11.2 71.7 all-gather.1
